TPU v7x, 128 devices: a whole 4x4x4 slice. The times are simulated.
128 devices in a mesh: lat: 32 (over z, y, core), chan: 4 (over x).
Axes of the slice: x: 4, y: 4, z: 4, core: 2. Of those that a mesh axis runs over, the one named last changes fastest.
Arguments:
- field: bfloat16 [32, 3, 2, 512, 4096], P('chan', None, None, 'lat'), may hold values from -6 to 6
- mix_weight: bfloat16 [32, 32], replicated, may hold values from -1 to 1
- spectral_gain: float32 [32, 2048], P('chan'), may hold values from 0.05 to 1
- legendre: bfloat16 [2, 512, 512, 1024], P(None, 'lat'), may hold values from -0.25 to 0.25
- slot_mode: int32 [512], replicated, may hold values from 0 to 511, as said below
Outputs:
- layered: bfloat16 [32, 3, 2, 512, 4096], P('chan', None, None, 'lat')
Inputs may be any that keep to these rules, and one draw needn't show every extreme that they name: `slot_mode`: A permutation of the mode indices; slots 2 j and 2 j + 1 carry the modes k and 511 - k for some k, so the slots of every index of lat carry whole such pairs.
All inputs are finite; a program needn't handle non-finite values.
Results may differ from a plain program's by a relative error of at most 0.0085.
Values may be sent and summed in bfloat16 or wider, within the bound.
No kernel may reach another device: no remote copies, remote signals or barrier semaphores. Data moves between devices by JAX's collectives and lax.ppermute only.
A program may use at most 192 MiB of HBM per device.

v0:
```python
import math
import jax
import jax.numpy as jnp
from jax import lax
from jax.sharding import PartitionSpec as P


def local(field, mix_weight, spectral_gain, legendre, slot_mode, n_lat, n_chan):
    chans = field.shape[0]
    fields = field.shape[1]
    cycles = field.shape[3]
    points = field.shape[4]
    total_modes = slot_mode.shape[0]
    degrees = spectral_gain.shape[1]
    half_deg = degrees // 2
    step_size = degrees // total_modes
    period = points // math.gcd(points, step_size)
    devices = n_lat * n_chan
    per_dev = total_modes // devices
    lat_index = lax.axis_index("lat")
    chan_index = lax.axis_index("chan")
    row_count = chans * fields * 2 * cycles
    modes = (slot_mode * step_size).reshape(n_lat, n_chan, per_dev)
    modes = jnp.transpose(modes, (1, 0, 2)).reshape(devices, 1, per_dev)
    quarter = jnp.array([0, points // 4], jnp.int32).reshape(1, 2, 1)
    lanes = min(128, period)
    blocks = period // lanes
    scale = 2.0 * math.pi / points
    hi_turns = (
        modes[..., None] * (lax.iota(jnp.int32, blocks) * lanes) + quarter[..., None]
    ) % points
    lo_turns = modes[..., None] * lax.iota(jnp.int32, lanes) % points
    hi_angle = hi_turns.astype(jnp.float32) * scale
    lo_angle = lo_turns.astype(jnp.float32) * scale
    ca, sa = (jnp.cos(hi_angle)[..., None], jnp.sin(hi_angle)[..., None])
    cb, sb = (jnp.cos(lo_angle)[..., None, :], jnp.sin(lo_angle)[..., None, :])
    basis = (ca * cb - sa * sb).reshape(-1, period)
    fwd = (basis * math.sqrt(2.0 / points)).astype(jnp.bfloat16)
    ratio = math.sqrt(points / (2.0 * total_modes))
    if ratio == 2.0 ** round(math.log2(ratio)):
        fwd = lax.optimization_barrier(fwd)
        inv = fwd
    else:
        inv = (basis * math.sqrt(1.0 / total_modes)).astype(jnp.bfloat16)
        ratio = 1.0
    flat = field.reshape(-1, points)
    summed = flat[:, :period].astype(jnp.float32)
    for n in range(1, points // period):
        summed = summed + flat[:, n * period : (n + 1) * period].astype(jnp.float32)
    high = summed.astype(jnp.bfloat16)
    low = (summed - high.astype(jnp.float32)).astype(jnp.bfloat16)
    rows = jnp.concatenate([high, low], axis=1)
    spec_t = lax.dot_general(
        jnp.concatenate([fwd, fwd], axis=1),
        rows,
        (((1,), (1,)), ((), ())),
        preferred_element_type=jnp.float32,
    ).astype(jnp.bfloat16)
    sent = spec_t.reshape(devices, 2 * per_dev, row_count)
    got = lax.all_to_all(sent, ("chan", "lat"), 0, 0, tiled=True)
    got = got.reshape(n_chan, n_lat, 2, per_dev, chans, fields, 2, cycles)
    sign = jnp.array([[1.0, 1.0], [1.0, -1.0]], jnp.float32)
    weight = mix_weight.astype(jnp.float32).reshape(-1, n_chan, chans)
    mix_fold = sign[:, None, None, :, None] * jnp.transpose(weight, (0, 2, 1))[None, :, :, None, :]
    mix_fold = mix_fold.astype(jnp.bfloat16)
    folded = jnp.einsum(
        "pokhC,CLqskthr->sptqoLr", mix_fold, got, preferred_element_type=jnp.float32
    ).astype(jnp.bfloat16)
    folded = folded.reshape(per_dev, 2, fields, 2, -1, n_lat * cycles)
    leg = lax.dynamic_slice_in_dim(legendre, chan_index * per_dev, per_dev, 1)
    coefficients = jnp.einsum(
        "sptqor,psri->sptqoi", folded, leg, preferred_element_type=jnp.float32
    )
    all_gain = lax.all_gather(spectral_gain, "chan", axis=0, tiled=True)
    gain_par = jnp.transpose(all_gain.reshape(-1, half_deg, 2), (2, 0, 1))
    own_modes = lax.dynamic_slice_in_dim(
        modes.reshape(-1), (chan_index * n_lat + lat_index) * per_dev, per_dev, 0
    )
    degree = 2 * lax.iota(jnp.int32, half_deg)[None, :] + lax.iota(jnp.int32, 2)[:, None]
    allowed = degree[None, :, :] >= own_modes[:, None, None]
    sign = jnp.array([[1.0, 1.0], [1.0, -1.0]], jnp.float32).reshape(1, 2, 2, 1, 1, 1, 1)
    scaled = gain_par[None, :, None, None, :, :] * coefficients
    filtered = jnp.where(
        allowed[:, None, :, None, None, None, :], sign * scaled[:, None], 0.0
    ).astype(jnp.bfloat16)
    back = jnp.einsum(
        "shptqoi,psri->shtqor", filtered, leg, preferred_element_type=jnp.float32
    ).astype(jnp.bfloat16)
    back = back.reshape(per_dev, 2, fields, 2, n_chan, chans, n_lat, cycles)
    leaving = jnp.transpose(back, (4, 6, 3, 0, 5, 2, 1, 7)).reshape(devices, 2 * per_dev, row_count)
    returned = lax.all_to_all(leaving, ("chan", "lat"), 0, 0, tiled=True)
    returned = returned.reshape(2 * total_modes, row_count)
    waveform = (
        lax.dot_general(returned, inv, (((0,), (0,)), ((), ())), preferred_element_type=jnp.float32)
        * ratio
    )
    waveform = waveform.reshape(chans, fields, -1, period)
    primal_h = waveform[:, 0]
    sigmoid_h = jax.nn.sigmoid(primal_h)
    slope_h = sigmoid_h * (1.0 + primal_h * (1.0 - sigmoid_h))
    gain_h = primal_h * sigmoid_h
    flat = field.reshape(chans, fields, -1, points)
    pieces = []
    for n in range(points // period):
        initial = flat[:, :, :, n * period : (n + 1) * period].astype(jnp.float32)
        primal = initial[:, 0] + gain_h
        tangents = initial[:, 1:] + slope_h[:, None] * waveform[:, 1:]
        pieces.append(jnp.concatenate([primal[:, None], tangents], axis=1).astype(jnp.bfloat16))
    out = jnp.concatenate(pieces, axis=3)
    return out.reshape(field.shape)


def solution(mesh):
    n_lat = mesh.shape["lat"]
    n_chan = mesh.shape["chan"]
    placed = (
        P("chan", None, None, "lat", None),
        P(),
        P("chan", None),
        P(None, "lat", None, None),
        P(),
    )

    def body(field, mix_weight, spectral_gain, legendre, slot_mode):
        return local(field, mix_weight, spectral_gain, legendre, slot_mode, n_lat, n_chan)

    return jax.shard_map(
        body,
        mesh=mesh,
        in_specs=placed,
        out_specs=P("chan", None, None, "lat", None),
        check_vma=False,
    )
```

profile of v0, /device:TPU:1, one launch (start us, length us, event | category | flops | bytes accessed | tf_op | source)
XLA Modules:
  0.0 178.5 jit_solution(10418024160867076549)
XLA Ops:
  0.0 0.7 broadcast_multiply_fusion.2
  1.2 2.4 %fusion.54 = (f32[128,4,128]{2,1,0:T(4,128)S(1)}, f32[128,4,128]{2,1,0:T(4,128)S(1)}) fusion(s32[128,4]{1,0:T(8,128)S(1)} %copy.59), kind=kLoop, calls=%fused_computation.66 | loop fusion | flops 917504 | bytes 526336 | tf_op jit(solution)/shard_map/cos | solution.py:36
  4.4 2.5 %multiply_convert_fusion = bf16[128,2,4,8,128]{4,3,2,1,0:T(8,128)(2,1)S(1)} fusion(f32[128,4,128]{2,1,0:T(4,128)S(1)} %get-tuple-element.21, f32[128,2,4,8]{3,2,1,0:T(4,128)S(1)} %copy.60, f32[128,4,128]{2,1,0:T(4,128)S(1)} %get-tuple-element.20, f32[128,2,4,8]{3,2,1,0:T(4,128)S(1)} %copy.58), kind=kLoop, calls=%fused_computation.21 | loop fusion | flops 5242880 | bytes 2686976 | tf_op jit(solution)/shard_map/convert_element_type | solution.py:38
  7.5 1.6 subtract_convert_fusion
  9.3 4.6 %fusion.39 = bf16[128,8,768]{2,1,0:T(8,128)(2,1)} fusion(bf16[768,1024]{1,0:T(8,128)(2,1)S(1)} %get-tuple-element.5, bf16[768,1024]{1,0:T(8,128)(2,1)S(1)} %get-tuple-element.6, bf16[1024,1024]{1,0:T(8,128)(2,1)S(1)} %bitcast.84), kind=kOutput, calls=%fused_computation.46 | convolution fusion | flops 3236691968 | bytes 6815744 | tf_op jit(solution)/shard_map/dot_general | solution.py:53
  13.9 11.5 %all-to-all-start = ((bf16[128,8,768]{2,1,0:T(8,128)(2,1)}), bf16[128,8,768]{2,1,0:T(8,128)(2,1)S(1)}, u32[]{:S(2)}, u32[]{:S(2)}) async-start(bf16[128,8,768]{2,1,0:T(8,128)(2,1)} %fusion.39), calls=%async_computation | async-start | bytes 3145728 | tf_op jit(solution)/shard_map/all_to_all | solution.py:60
  25.7 25.3 %all_gather.3 = f32[32,2048]{1,0:T(8,128)S(1)} all-gather(f32[8,2048]{1,0:T(8,128)S(1)} %copy-done.5), channel_id=1, replica_groups=mesh['lat'=32,'chan'=4] {'chan'}, dimensions={0}, use_global_device_ids=true | all-gather | bytes 327680 | tf_op jit(solution)/shard_map/all_gather | solution.py:74
  52.0 1.2 copy.61
  53.2 4.6 %reshape.168 = bf16[4,32,2,4,8,3,2,16]{1,0,7,6,5,4,3,2:T(4,128)(2,1)} reshape(bf16[128,8,768]{0,2,1:T(8,128)(2,1)S(1)} %copy.61) | data formatting | bytes 3145728 | tf_op jit(solution)/shard_map/reshape | solution.py:61
  57.8 9.6 %fusion.6 = bf16[4,2,3,2,32,32,16]{4,5,1,6,2,0,3:T(8,128)(2,1)} fusion(f32[32,8,4]{0,2,1:T(4,128)S(1)} %copy.63, f32[2,2]{1,0:T(2,128)S(1)} %copy-done.7, bf16[4,32,2,4,8,3,2,16]{1,0,7,6,5,4,3,2:T(4,128)(2,1)} %reshape.168), kind=kOutput, calls=%fused_computation.8 | convolution fusion | flops 101457920 | bytes 3149840 | tf_op jit(solution)/shard_map/pokhC,CLqskthr->sptqoLr/dot_general | solution.py:66
  67.3 10.1 %copy.65 = bf16[4,2,3,2,32,32,16]{4,6,5,3,2,1,0:T(8,128)(2,1)S(1)} copy(bf16[4,2,3,2,32,32,16]{4,5,1,6,2,0,3:T(8,128)(2,1)} %fusion.6) | data formatting | bytes 3145728 | tf_op jit(solution)/shard_map/convert_element_type | solution.py:68
  77.4 8.6 %broadcast_multiply_fusion = f32[4,2,3,2,32,1024]{5,4,1,3,2,0:T(8,128)} fusion(f32[2,32,1024]{2,1,0:T(8,128)S(1)} %copy.56, bf16[4,2,3,2,32,512]{4,5,3,2,1,0:T(8,128)(2,1)S(1)} %bitcast.80, bf16[2,16,512,1024]{3,2,1,0:T(8,128)(2,1)} %param.11, s32[]{:T(128)S(6)} %select_n.43), kind=kOutput, calls=%fused_computation.28 | convolution fusion | flops 1612185600 | bytes 16515076 | tf_op jit(solution)/shard_map/sptqor,psri->sptqoi/dot_general | solution.py:71
  86.0 8.7 %bitcast_convert_fusion.1 = bf16[4,2,3,2,32,512]{5,4,3,2,1,0:T(8,128)(2,1)S(1)} fusion(f32[4,2,3,2,32,1024]{5,4,1,3,2,0:T(8,128)} %broadcast_multiply_fusion, f32[2,2]{1,0:T(2,128)S(1)} %copy-done.7, pred[4,2,1024]{2,1,0:T(4,128)(4,1)S(1)} %broadcast_compare_fusion, bf16[2,16,512,1024]{3,2,1,0:T(8,128)(2,1)} %param.11, s32[]{:T(128)S(6)} %select_n.43), kind=kOutput, calls=%fused_computation.25 | convolution fusion | flops 3231449088 | bytes 16261140 | tf_op jit(solution)/shard_map/shptqoi,psri->shtqor/dot_general | solution.py:86
  94.7 11.9 %reshape.171 = bf16[4,2,3,2,4,8,32,16]{7,6,5,4,3,2,1,0:T(8,128)(2,1)} reshape(bf16[4,2,3,2,32,512]{5,4,3,2,1,0:T(8,128)(2,1)S(1)} %bitcast_convert_fusion.1) | data formatting | bytes 3145728 | tf_op jit(solution)/shard_map/reshape | solution.py:89
  106.5 14.5 %copy.68 = bf16[4,32,2,4,8,3,2,16]{1,0,7,6,5,4,3,2:T(4,128)(2,1)} copy(bf16[4,32,2,4,8,3,2,16]{7,1,4,0,2,5,6,3:T(8,128)(2,1)} %bitcast.77) | data formatting | bytes 3145728 | tf_op jit(solution)/shard_map/transpose | solution.py:90
  121.0 7.3 %reshape.172 = bf16[128,8,768]{0,2,1:T(8,128)(2,1)S(1)} reshape(bf16[4,32,2,4,8,3,2,16]{1,0,7,6,5,4,3,2:T(4,128)(2,1)} %copy.68) | data formatting | bytes 3145728 | tf_op jit(solution)/shard_map/reshape | solution.py:90
  128.3 2.0 %copy.69 = bf16[128,8,768]{2,1,0:T(8,128)(2,1)} copy(bf16[128,8,768]{0,2,1:T(8,128)(2,1)S(1)} %reshape.172) | data formatting | bytes 3145728 | tf_op jit(solution)/shard_map/reshape | solution.py:90
  130.3 10.3 %all-to-all-start.1 = ((bf16[128,8,768]{2,1,0:T(8,128)(2,1)}), bf16[128,8,768]{2,1,0:T(8,128)(2,1)}, u32[]{:S(2)}, u32[]{:S(2)}) async-start(bf16[128,8,768]{2,1,0:T(8,128)(2,1)} %copy.69), calls=%async_computation.1 | async-start | bytes 3145728 | tf_op jit(solution)/shard_map/all_to_all | solution.py:91
  140.6 7.2 %slice_convert_fusion.3 = (f32[8,3,32,1024]{3,2,1,0:T(8,128)S(1)}, f32[8,3,32,1024]{3,2,1,0:T(8,128)}, f32[8,3,32,1024]{3,2,1,0:T(8,128)}, f32[8,3,32,1024]{3,2,1,0:T(8,128)}) fusion(bf16[8,3,32,4096]{3,2,1,0:T(8,128)(2,1)} %bitcast.78), kind=kLoop, calls=%fused_computation.44 | loop fusion | flops 3145728 | bytes 18874368 | tf_op jit(solution)/shard_map/convert_element_type | solution.py:105
  147.8 17.2 %all-to-all-done.1 = bf16[128,8,768]{2,1,0:T(8,128)(2,1)} async-done(((bf16[128,8,768]{2,1,0:T(8,128)(2,1)}), bf16[128,8,768]{2,1,0:T(8,128)(2,1)}, u32[]{:S(2)}, u32[]{:S(2)}) %all-to-all-start.1) | async-done | bytes 1572896 | tf_op jit(solution)/shard_map/all_to_all | solution.py:91
  165.0 4.1 %convolution_multiply_fusion = f32[768,1024]{1,0:T(8,128)S(1)} fusion(bf16[1024,1024]{1,0:T(8,128)(2,1)} %bitcast.85, bf16[128,8,768]{2,1,0:T(8,128)(2,1)} %all-to-all-done.1), kind=kOutput, calls=%fused_computation.39 | convolution fusion | flops 1611399168 | bytes 6815744 | tf_op jit(solution)/shard_map/dot_general | solution.py:94
  169.1 3.1 %fusion.47 = (bf16[8,1,32,1024]{3,2,1,0:T(8,128)(2,1)S(1)}, bf16[8,1,32,1024]{3,2,1,0:T(8,128)(2,1)S(1)}, bf16[8,1,32,1024]{3,2,1,0:T(8,128)(2,1)}, bf16[8,1,32,1024]{3,2,1,0:T(8,128)(2,1)}, f32[8,32,1024]{2,1,0:T(8,128)S(1)}) fusion(f32[8,3,32,1024]{3,2,1,0:T(8,128)S(1)} %get-tuple-element.7, f32[8,3,32,1024]{3,2,1,0:T(8,128)S(1)} %bitcast.81, ...), kind=kLoop, calls=%fused_computation.54 | loop fusion | flops 4194304 | bytes 8388608 | tf_op jit(solution)/shard_map/convert.17
  172.3 1.7 fusion.30
  173.9 4.6 %maximum_maximum_fusion = bf16[8,3,2,16,4096]{4,3,2,1,0:T(8,128)(2,1)} fusion(bf16[8,2,2,16,1024]{4,3,2,1,0:T(8,128)(2,1)S(1)} %bitcast.90, bf16[8,1,2,16,1024]{4,3,2,1,0:T(8,128)(2,1)} %bitcast.94, bf16[8,2,2,16,1024]{4,3,2,1,0:T(8,128)(2,1)S(1)} %bitcast.89, bf16[8,1,2,16,1024]{4,3,2,1,0:T(8,128)(2,1)} %bitcast.93, ...), kind=kLoop, calls=%fused_computation.9 | loop fusion | flops 50331648 | bytes 12582912 | tf_op jit(solution)/shard_map/concatenate | solution.py:109
  (39 shorter events, 3.3 us)
Async XLA Ops:
  4.4 3.1 %copy-start = (bf16[8,3,2,16,4096]{4,3,2,1,0:T(8,128)(2,1)S(1)}, bf16[8,3,2,16,4096]{4,3,2,1,0:T(8,128)(2,1)}, u32[]{:S(2)}) copy-start(bf16[8,3,2,16,4096]{4,3,2,1,0:T(8,128)(2,1)} %param.8) | copy-start | bytes 18874372
  7.5 1.8 %copy-start.4 = (bf16[128,8,8,128]{3,1,2,0:T(8,128)(2,1)}, bf16[128,8,8,128]{3,1,2,0:T(8,128)(2,1)S(1)}, u32[]{:S(2)}) copy-start(bf16[128,8,8,128]{3,1,2,0:T(8,128)(2,1)S(1)} %copy.103) | copy-start | bytes 6291460
  9.3 16.1 %copy-start.6 = (bf16[32,32]{1,0:T(8,128)(2,1)S(1)}, bf16[32,32]{1,0:T(8,128)(2,1)}, u32[]{:S(2)}) copy-start(bf16[32,32]{1,0:T(8,128)(2,1)} %param.9) | copy-start | bytes 6148
  9.3 16.4 %copy-start.5 = (f32[8,2048]{1,0:T(8,128)S(1)}, f32[8,2048]{1,0:T(8,128)}, u32[]{:S(2)}) copy-start(f32[8,2048]{1,0:T(8,128)} %param.10) | copy-start | bytes 196612
  13.9 38.0 %all-to-all-start = ((bf16[128,8,768]{2,1,0:T(8,128)(2,1)}), bf16[128,8,768]{2,1,0:T(8,128)(2,1)S(1)}, u32[]{:S(2)}, u32[]{:S(2)}) async-start(bf16[128,8,768]{2,1,0:T(8,128)(2,1)} %fusion.39), calls=%async_computation | async-start | bytes 3145728 | tf_op jit(solution)/shard_map/all_to_all | solution.py:60
  53.1 4.6 %copy-start.7 = (f32[2,2]{1,0:T(2,128)S(1)}, f32[2,2]{1,0:T(2,128)}, u32[]{:S(2)}) copy-start(f32[2,2]{1,0:T(2,128)} %constant.63.clone) | copy-start | bytes 52
  130.3 34.7 %all-to-all-start.1 = ((bf16[128,8,768]{2,1,0:T(8,128)(2,1)}), bf16[128,8,768]{2,1,0:T(8,128)(2,1)}, u32[]{:S(2)}, u32[]{:S(2)}) async-start(bf16[128,8,768]{2,1,0:T(8,128)(2,1)} %copy.69), calls=%async_computation.1 | async-start | bytes 3145728 | tf_op jit(solution)/shard_map/all_to_all | solution.py:91
  165.0 4.1 %copy-start.1 = (f32[8,3,32,1024]{3,2,1,0:T(8,128)S(1)}, f32[8,3,32,1024]{3,2,1,0:T(8,128)}, u32[]{:S(2)}) copy-start(f32[8,3,32,1024]{3,2,1,0:T(8,128)} %get-tuple-element.8) | copy-start | bytes 9437188
  165.0 4.1 %copy-start.2 = (f32[8,3,32,1024]{3,2,1,0:T(8,128)S(1)}, f32[8,3,32,1024]{3,2,1,0:T(8,128)}, u32[]{:S(2)}) copy-start(f32[8,3,32,1024]{3,2,1,0:T(8,128)} %get-tuple-element.9) | copy-start | bytes 9437188
  169.1 3.2 %copy-start.3 = (f32[8,3,32,1024]{3,2,1,0:T(8,128)S(1)}, f32[8,3,32,1024]{3,2,1,0:T(8,128)}, u32[]{:S(2)}) copy-start(f32[8,3,32,1024]{3,2,1,0:T(8,128)} %get-tuple-element.10) | copy-start | bytes 9437188
where the time goes:
time: 179 us
  local copies, waits for them, and re-layouts  54.3 us (30%)
  matrix products  35.5 us (20%)
  blocking collectives  25.3 us (14%)
  other arithmetic  24.1 us (13%)
  starting transfers between devices  21.8 us (12%)
  waiting for transfers between devices  17.2 us (10%)
    all_gather x1, blocking collectives, local(): all_gain = lax.all_gather(spectral_gain, 'chan', axis=0, tiled=True)  25.3 us
    all_to_all x1, waiting for transfers between devices, local(): returned = lax.all_to_all(leaving, ('chan', 'lat'), 0, 0, tiled=True)  17.2 us
    transpose x1, local copies, waits for them, and re-layouts, local(): jnp.transpose(back, (4, 6, 3, 0, 5, 2, 1, 7))  14.5 us
    reshape x1, local copies, waits for them, and re-layouts, local(): back = back.reshape(per_dev, 2, fields, 2, n_chan, chans, n_lat, cycles)  11.9 us
    all_to_all x1, starting transfers between devices, local(): got = lax.all_to_all(sent, ('chan', 'lat'), 0, 0, tiled=True)  11.5 us
    all_to_all x1, starting transfers between devices, local(): returned = lax.all_to_all(leaving, ('chan', 'lat'), 0, 0, tiled=True)  10.3 us
    convert_element_type x1, local copies, waits for them, and re-layouts, local(): folded = jnp.einsum('pokhC,CLqskthr->sptqoLr', mix_fold, got, preferred_e...  10.1 us
    dot_general x1, matrix products, local(): jnp.einsum('pokhC,CLqskthr->sptqoLr', mix_fold, got, preferred_element_ty...  9.56 us
  transfers between devices with their start and end apart: 2, of which 1 were waited for; matrix products, arithmetic and copies ran while one was open for 5% of the time, Pallas kernels for 0%

commit v1 on v0

--- a/solution.py
+++ b/solution.py
@@ -71,7 +71,9 @@
     coefficients = jnp.einsum(
         "sptqor,psri->sptqoi", folded, leg, preferred_element_type=jnp.float32
     )
-    all_gain = lax.all_gather(spectral_gain, "chan", axis=0, tiled=True)
+    all_gain = jnp.concatenate(
+        lax.all_to_all(jnp.stack([spectral_gain] * lax.axis_size("chan")), "chan", 0, 0), axis=0
+    )
     gain_par = jnp.transpose(all_gain.reshape(-1, half_deg, 2), (2, 0, 1))
     own_modes = lax.dynamic_slice_in_dim(
         modes.reshape(-1), (chan_index * n_lat + lat_index) * per_dev, per_dev, 0

time: 179 us -> 180 us (level)
  blocking collectives: 25.3 us -> 0 us
  waiting for transfers between devices: 17.2 us -> 33.9 us
  local copies, waits for them, and re-layouts: 54.3 us -> 62.9 us
    all_gather x1 -> x0, blocking collectives: 25.3 us -> none  [local(): all_gain = lax.all_gather(spectral_gain, 'chan', axis=0, tiled=True)]
    all_to_all x1, waiting for transfers between devices: 0.01 us -> 16.5 us  [local(): got = lax.all_to_all(sent, ('chan', 'lat'), 0, 0, tiled=True)]
    another operation x0 -> x2, local copies, waits for them, and re-layouts: none -> 5.84 us  [the longest x1 4.28 us: local(): gain_par = jnp.transpose(all_gain.reshape(-1, half_deg, 2), (2, 0, 1))]
    all_to_all x0 -> x1, starting transfers between devices: none -> 4.84 us  [local(): lax.all_to_all(jnp.stack([spectral_gain] * lax.axis_size('chan')), 'chan'...]
    all_to_all x1, starting transfers between devices: 10.3 us -> 5.6 us  [local(): returned = lax.all_to_all(leaving, ('chan', 'lat'), 0, 0, tiled=True)]
    all_to_all x0 -> x1, local copies, waits for them, and re-layouts: none -> 3 us  [local(): lax.all_to_all(jnp.stack([spectral_gain] * lax.axis_size('chan')), 'chan'...]
  transfers between devices with their start and end apart: 2 -> 3, of which waited for: 1 -> 2; matrix products, arithmetic and copies ran while one was open for 5% -> 16% of each run, Pallas kernels for 0% -> 0%
where the time goes in v1:
time: 180 us; the launch traced here: 178 us
  local copies, waits for them, and re-layouts  62.9 us (35%)
  matrix products  35.5 us (20%)
  waiting for transfers between devices  33.9 us (19%)
  other arithmetic  24.1 us (13%)
  starting transfers between devices  21.9 us (12%)
    all_to_all x1, waiting for transfers between devices, local(): returned = lax.all_to_all(leaving, ('chan', 'lat'), 0, 0, tiled=True)  17.3 us
    all_to_all x1, waiting for transfers between devices, local(): got = lax.all_to_all(sent, ('chan', 'lat'), 0, 0, tiled=True)  16.5 us
    transpose x1, local copies, waits for them, and re-layouts, local(): jnp.transpose(back, (4, 6, 3, 0, 5, 2, 1, 7))  14.5 us
    reshape x1, local copies, waits for them, and re-layouts, local(): back = back.reshape(per_dev, 2, fields, 2, n_chan, chans, n_lat, cycles)  11.9 us
    all_to_all x1, starting transfers between devices, local(): got = lax.all_to_all(sent, ('chan', 'lat'), 0, 0, tiled=True)  11.5 us
    convert_element_type x1, local copies, waits for them, and re-layouts, local(): folded = jnp.einsum('pokhC,CLqskthr->sptqoLr', mix_fold, got, preferred_e...  10.1 us
    dot_general x1, matrix products, local(): jnp.einsum('pokhC,CLqskthr->sptqoLr', mix_fold, got, preferred_element_ty...  9.56 us
    reshape x2, local copies, waits for them, and re-layouts, local(): jnp.transpose(back, (4, 6, 3, 0, 5, 2, 1, 7))  9.33 us
  transfers between devices with their start and end apart: 3, of which 2 were waited for; matrix products, arithmetic and copies ran while one was open for 16% of the time, Pallas kernels for 0%

profile of v1, /device:TPU:1, one launch (start us, length us, event | category | flops | bytes accessed | tf_op | source)
XLA Modules:
  0.0 178.5 jit_solution(11095630476859552604)
XLA Ops:
  1.6 4.8 %all-to-all-start = ((f32[4,8,2048]{2,1,0:T(8,128)}), f32[4,8,2048]{2,1,0:T(8,128)S(1)}, u32[]{:S(2)}, u32[]{:S(2)}) async-start(f32[4,8,2048]{2,1,0:T(8,128)} %stack.2), calls=%async_computation | async-start | bytes 524288 | tf_op jit(solution)/shard_map/all_to_all | solution.py:75
  7.6 2.4 %fusion.54 = (f32[128,4,128]{2,1,0:T(4,128)S(1)}, f32[128,4,128]{2,1,0:T(4,128)S(1)}) fusion(s32[128,4]{1,0:T(8,128)S(1)} %copy.58), kind=kLoop, calls=%fused_computation.66 | loop fusion | flops 917504 | bytes 526336 | tf_op jit(solution)/shard_map/cos | solution.py:36
  10.8 2.5 %multiply_convert_fusion = bf16[128,2,4,8,128]{4,3,2,1,0:T(8,128)(2,1)S(1)} fusion(f32[128,4,128]{2,1,0:T(4,128)S(1)} %get-tuple-element.21, f32[128,2,4,8]{3,2,1,0:T(4,128)S(1)} %copy.59, f32[128,4,128]{2,1,0:T(4,128)S(1)} %get-tuple-element.20, f32[128,2,4,8]{3,2,1,0:T(4,128)S(1)} %copy.57), kind=kLoop, calls=%fused_computation.21 | loop fusion | flops 5242880 | bytes 2686976 | tf_op jit(solution)/shard_map/convert_element_type | solution.py:38
  15.7 4.6 %fusion.39 = bf16[128,8,768]{2,1,0:T(8,128)(2,1)} fusion(bf16[768,1024]{1,0:T(8,128)(2,1)S(1)} %get-tuple-element.5, bf16[768,1024]{1,0:T(8,128)(2,1)S(1)} %get-tuple-element.6, bf16[1024,1024]{1,0:T(8,128)(2,1)S(1)} %bitcast.84), kind=kOutput, calls=%fused_computation.46 | convolution fusion | flops 3236691968 | bytes 6815744 | tf_op jit(solution)/shard_map/dot_general | solution.py:53
  20.3 11.5 %all-to-all-start.1 = ((bf16[128,8,768]{2,1,0:T(8,128)(2,1)}), bf16[128,8,768]{2,1,0:T(8,128)(2,1)S(1)}, u32[]{:S(2)}, u32[]{:S(2)}) async-start(bf16[128,8,768]{2,1,0:T(8,128)(2,1)} %fusion.39), calls=%async_computation.1 | async-start | bytes 3145728 | tf_op jit(solution)/shard_map/all_to_all | solution.py:60
  32.2 3.0 %copy.54 = f32[4,8,2048]{1,0,2:T(4,128)} copy(f32[4,8,2048]{2,1,0:T(8,128)S(1)} %all-to-all-done) | data formatting | bytes 524288 | tf_op jit(solution)/shard_map/all_to_all | solution.py:75
  35.2 4.3 %reshape_reshape.7 = f32[32,1024,2]{0,2,1:T(2,128)S(1)} reshape(f32[4,8,2048]{1,0,2:T(4,128)} %copy.54) | data formatting | bytes 524288 | tf_op jit(solution)/shard_map/reshape;reshape | solution.py:77
  40.0 16.5 %all-to-all-done.1 = bf16[128,8,768]{2,1,0:T(8,128)(2,1)S(1)} async-done(((bf16[128,8,768]{2,1,0:T(8,128)(2,1)}), bf16[128,8,768]{2,1,0:T(8,128)(2,1)S(1)}, u32[]{:S(2)}, u32[]{:S(2)}) %all-to-all-start.1) | async-done | bytes 1572896 | tf_op jit(solution)/shard_map/all_to_all | solution.py:60
  57.7 4.6 %reshape.166 = bf16[4,32,2,4,8,3,2,16]{1,0,7,6,5,4,3,2:T(4,128)(2,1)} reshape(bf16[128,8,768]{0,2,1:T(8,128)(2,1)S(1)} %copy.60) | data formatting | bytes 3145728 | tf_op jit(solution)/shard_map/reshape | solution.py:61
  62.3 9.6 %fusion.6 = bf16[4,2,3,2,32,32,16]{4,5,1,6,2,0,3:T(8,128)(2,1)} fusion(f32[32,8,4]{0,2,1:T(4,128)S(1)} %copy.62, f32[2,2]{1,0:T(2,128)S(1)} %copy-done.6, bf16[4,32,2,4,8,3,2,16]{1,0,7,6,5,4,3,2:T(4,128)(2,1)} %reshape.166), kind=kOutput, calls=%fused_computation.8 | convolution fusion | flops 101457920 | bytes 3149840 | tf_op jit(solution)/shard_map/pokhC,CLqskthr->sptqoLr/dot_general | solution.py:66
  71.9 10.1 %copy.64 = bf16[4,2,3,2,32,32,16]{4,6,5,3,2,1,0:T(8,128)(2,1)S(1)} copy(bf16[4,2,3,2,32,32,16]{4,5,1,6,2,0,3:T(8,128)(2,1)} %fusion.6) | data formatting | bytes 3145728 | tf_op jit(solution)/shard_map/convert_element_type | solution.py:68
  81.9 8.6 %broadcast_multiply_fusion = f32[4,2,3,2,32,1024]{5,4,1,3,2,0:T(8,128)} fusion(f32[2,32,1024]{2,1,0:T(8,128)S(1)} %copy.55, bf16[4,2,3,2,32,512]{4,5,3,2,1,0:T(8,128)(2,1)S(1)} %bitcast.80, bf16[2,16,512,1024]{3,2,1,0:T(8,128)(2,1)} %param.11, s32[]{:T(128)S(6)} %select_n.43), kind=kOutput, calls=%fused_computation.28 | convolution fusion | flops 1612185600 | bytes 16515076 | tf_op jit(solution)/shard_map/sptqor,psri->sptqoi/dot_general | solution.py:71
  90.5 8.7 %bitcast_convert_fusion.1 = bf16[4,2,3,2,32,512]{5,4,3,2,1,0:T(8,128)(2,1)S(1)} fusion(f32[4,2,3,2,32,1024]{5,4,1,3,2,0:T(8,128)} %broadcast_multiply_fusion, f32[2,2]{1,0:T(2,128)S(1)} %copy-done.6, pred[4,2,1024]{2,1,0:T(4,128)(4,1)S(1)} %broadcast_compare_fusion, bf16[2,16,512,1024]{3,2,1,0:T(8,128)(2,1)} %param.11, s32[]{:T(128)S(6)} %select_n.43), kind=kOutput, calls=%fused_computation.25 | convolution fusion | flops 3231449088 | bytes 16261140 | tf_op jit(solution)/shard_map/shptqoi,psri->shtqor/dot_general | solution.py:88
  99.2 11.9 %reshape.169 = bf16[4,2,3,2,4,8,32,16]{7,6,5,4,3,2,1,0:T(8,128)(2,1)} reshape(bf16[4,2,3,2,32,512]{5,4,3,2,1,0:T(8,128)(2,1)S(1)} %bitcast_convert_fusion.1) | data formatting | bytes 3145728 | tf_op jit(solution)/shard_map/reshape | solution.py:91
  111.0 14.5 %copy.67 = bf16[4,32,2,4,8,3,2,16]{1,0,7,6,5,4,3,2:T(4,128)(2,1)} copy(bf16[4,32,2,4,8,3,2,16]{7,1,4,0,2,5,6,3:T(8,128)(2,1)} %bitcast.77) | data formatting | bytes 3145728 | tf_op jit(solution)/shard_map/transpose | solution.py:92
  125.5 7.3 %reshape.170 = bf16[128,8,768]{0,2,1:T(8,128)(2,1)S(1)} reshape(bf16[4,32,2,4,8,3,2,16]{1,0,7,6,5,4,3,2:T(4,128)(2,1)} %copy.67) | data formatting | bytes 3145728 | tf_op jit(solution)/shard_map/reshape | solution.py:92
  132.8 2.0 %copy.68 = bf16[128,8,768]{2,1,0:T(8,128)(2,1)} copy(bf16[128,8,768]{0,2,1:T(8,128)(2,1)S(1)} %reshape.170) | data formatting | bytes 3145728 | tf_op jit(solution)/shard_map/reshape | solution.py:92
  134.8 5.6 %all-to-all-start.2 = ((bf16[128,8,768]{2,1,0:T(8,128)(2,1)}), bf16[128,8,768]{2,1,0:T(8,128)(2,1)}, u32[]{:S(2)}, u32[]{:S(2)}) async-start(bf16[128,8,768]{2,1,0:T(8,128)(2,1)} %copy.68), calls=%async_computation.2 | async-start | bytes 3145728 | tf_op jit(solution)/shard_map/all_to_all | solution.py:93
  140.5 7.2 %slice_convert_fusion.3 = (f32[8,3,32,1024]{3,2,1,0:T(8,128)S(1)}, f32[8,3,32,1024]{3,2,1,0:T(8,128)}, f32[8,3,32,1024]{3,2,1,0:T(8,128)}, f32[8,3,32,1024]{3,2,1,0:T(8,128)}) fusion(bf16[8,3,32,4096]{3,2,1,0:T(8,128)(2,1)} %bitcast.78), kind=kLoop, calls=%fused_computation.44 | loop fusion | flops 3145728 | bytes 18874368 | tf_op jit(solution)/shard_map/convert_element_type | solution.py:107
  147.6 17.3 %all-to-all-done.2 = bf16[128,8,768]{2,1,0:T(8,128)(2,1)} async-done(((bf16[128,8,768]{2,1,0:T(8,128)(2,1)}), bf16[128,8,768]{2,1,0:T(8,128)(2,1)}, u32[]{:S(2)}, u32[]{:S(2)}) %all-to-all-start.2) | async-done | bytes 1572896 | tf_op jit(solution)/shard_map/all_to_all | solution.py:93
  165.0 4.1 %convolution_multiply_fusion = f32[768,1024]{1,0:T(8,128)S(1)} fusion(bf16[1024,1024]{1,0:T(8,128)(2,1)} %bitcast.85, bf16[128,8,768]{2,1,0:T(8,128)(2,1)} %all-to-all-done.2), kind=kOutput, calls=%fused_computation.39 | convolution fusion | flops 1611399168 | bytes 6815744 | tf_op jit(solution)/shard_map/dot_general | solution.py:96
  169.1 3.1 %fusion.47 = (bf16[8,1,32,1024]{3,2,1,0:T(8,128)(2,1)S(1)}, bf16[8,1,32,1024]{3,2,1,0:T(8,128)(2,1)S(1)}, bf16[8,1,32,1024]{3,2,1,0:T(8,128)(2,1)}, bf16[8,1,32,1024]{3,2,1,0:T(8,128)(2,1)}, f32[8,32,1024]{2,1,0:T(8,128)S(1)}) fusion(f32[8,3,32,1024]{3,2,1,0:T(8,128)S(1)} %get-tuple-element.7, f32[8,3,32,1024]{3,2,1,0:T(8,128)S(1)} %bitcast.81, ...), kind=kLoop, calls=%fused_computation.54 | loop fusion | flops 4194304 | bytes 8388608 | tf_op jit(solution)/shard_map/convert.17
  172.2 1.7 fusion.30
  173.9 4.6 %maximum_maximum_fusion = bf16[8,3,2,16,4096]{4,3,2,1,0:T(8,128)(2,1)} fusion(bf16[8,2,2,16,1024]{4,3,2,1,0:T(8,128)(2,1)S(1)} %bitcast.90, bf16[8,1,2,16,1024]{4,3,2,1,0:T(8,128)(2,1)} %bitcast.94, bf16[8,2,2,16,1024]{4,3,2,1,0:T(8,128)(2,1)S(1)} %bitcast.89, bf16[8,1,2,16,1024]{4,3,2,1,0:T(8,128)(2,1)} %bitcast.93, ...), kind=kLoop, calls=%fused_computation.9 | loop fusion | flops 50331648 | bytes 12582912 | tf_op jit(solution)/shard_map/concatenate | solution.py:111
  (40 shorter events, 7.9 us)
Async XLA Ops:
  1.6 18.8 %all-to-all-start = ((f32[4,8,2048]{2,1,0:T(8,128)}), f32[4,8,2048]{2,1,0:T(8,128)S(1)}, u32[]{:S(2)}, u32[]{:S(2)}) async-start(f32[4,8,2048]{2,1,0:T(8,128)} %stack.2), calls=%async_computation | async-start | bytes 524288 | tf_op jit(solution)/shard_map/all_to_all | solution.py:75
  10.8 3.1 %copy-start = (bf16[8,3,2,16,4096]{4,3,2,1,0:T(8,128)(2,1)S(1)}, bf16[8,3,2,16,4096]{4,3,2,1,0:T(8,128)(2,1)}, u32[]{:S(2)}) copy-start(bf16[8,3,2,16,4096]{4,3,2,1,0:T(8,128)(2,1)} %param.8) | copy-start | bytes 18874372
  13.9 1.8 %copy-start.4 = (bf16[128,8,8,128]{3,1,2,0:T(8,128)(2,1)}, bf16[128,8,8,128]{3,1,2,0:T(8,128)(2,1)S(1)}, u32[]{:S(2)}) copy-start(bf16[128,8,8,128]{3,1,2,0:T(8,128)(2,1)S(1)} %copy.102) | copy-start | bytes 6291460
  15.7 16.1 %copy-start.5 = (bf16[32,32]{1,0:T(8,128)(2,1)S(1)}, bf16[32,32]{1,0:T(8,128)(2,1)}, u32[]{:S(2)}) copy-start(bf16[32,32]{1,0:T(8,128)(2,1)} %param.9) | copy-start | bytes 6148
  20.3 36.2 %all-to-all-start.1 = ((bf16[128,8,768]{2,1,0:T(8,128)(2,1)}), bf16[128,8,768]{2,1,0:T(8,128)(2,1)S(1)}, u32[]{:S(2)}, u32[]{:S(2)}) async-start(bf16[128,8,768]{2,1,0:T(8,128)(2,1)} %fusion.39), calls=%async_computation.1 | async-start | bytes 3145728 | tf_op jit(solution)/shard_map/all_to_all | solution.py:60
  57.7 4.6 %copy-start.6 = (f32[2,2]{1,0:T(2,128)S(1)}, f32[2,2]{1,0:T(2,128)}, u32[]{:S(2)}) copy-start(f32[2,2]{1,0:T(2,128)} %constant.63.clone) | copy-start | bytes 52
  134.8 30.1 %all-to-all-start.2 = ((bf16[128,8,768]{2,1,0:T(8,128)(2,1)}), bf16[128,8,768]{2,1,0:T(8,128)(2,1)}, u32[]{:S(2)}, u32[]{:S(2)}) async-start(bf16[128,8,768]{2,1,0:T(8,128)(2,1)} %copy.68), calls=%async_computation.2 | async-start | bytes 3145728 | tf_op jit(solution)/shard_map/all_to_all | solution.py:93
  165.0 4.1 %copy-start.1 = (f32[8,3,32,1024]{3,2,1,0:T(8,128)S(1)}, f32[8,3,32,1024]{3,2,1,0:T(8,128)}, u32[]{:S(2)}) copy-start(f32[8,3,32,1024]{3,2,1,0:T(8,128)} %get-tuple-element.8) | copy-start | bytes 9437188
  165.0 4.1 %copy-start.2 = (f32[8,3,32,1024]{3,2,1,0:T(8,128)S(1)}, f32[8,3,32,1024]{3,2,1,0:T(8,128)}, u32[]{:S(2)}) copy-start(f32[8,3,32,1024]{3,2,1,0:T(8,128)} %get-tuple-element.9) | copy-start | bytes 9437188
  169.1 3.1 %copy-start.3 = (f32[8,3,32,1024]{3,2,1,0:T(8,128)S(1)}, f32[8,3,32,1024]{3,2,1,0:T(8,128)}, u32[]{:S(2)}) copy-start(f32[8,3,32,1024]{3,2,1,0:T(8,128)} %get-tuple-element.10) | copy-start | bytes 9437188
